TPU v7x, 256 devices: a whole 4x4x8 slice. The times are simulated.
256 devices in a mesh: sect: 2 (over y_lo), batch: 16 (over z, core), head: 8 (over x, y_hi).
Axes of the slice: x: 4, y: 4 (y_hi: 2, y_lo: 2; y = y_hi * 2 + y_lo), z: 8, core: 2. Of those that a mesh axis runs over, the one named last changes fastest.
Arguments:
- queries: bfloat16 [96, 16, 512], P('batch', 'head', 'sect'), may hold values from -51 to 51
- newest_key_value: bfloat16 [96, 4, 256], P('batch'), may hold values from -5 to 5
- page_cache: bfloat16 [96, 256, 64, 256], P('batch', ('sect', 'head')), may hold values from -4 to 4
- lengths: int32 [96], P('batch'), may hold values from 2048 to 4096, as said below
- page_ids: int32 [96, 4, 32], P('batch'), may hold values from 0 to 63, as said below
- out_weight: bfloat16 [8192, 4096], P(('sect', 'head'), 'batch'), may hold values from -0.0625 to 0.0625
- residual: bfloat16 [96, 4096], P(None, 'batch'), may hold values from -2 to 2
- norm_gain: float32 [4096], P('batch'), may hold values from 0.25 to 1.75
- expert_ids: int32 [96, 8], replicated, may hold values from 0 to 63, all different within a row; in each aligned block of 96 rows (0 to 95, 96 to 191, ...) at most 24 rows name the same one
- route_weight: float32 [96, 8], replicated, may hold values from 0.1 to 1
- gate_up_weight: bfloat16 [32, 4096, 2, 3072], P(('sect', 'batch'), None, None, 'head'), may hold values from -0.09375 to 0.09375
- down_weight: bfloat16 [32, 3072, 4096], P(('sect', 'batch'), 'head'), may hold values from -0.15625 to 0.15625
Outputs:
- layer_out: bfloat16 [96, 4096], P(None, 'batch')
Inputs may be any that keep to these rules, and one draw needn't show every extreme that they name: `lengths`: some sequence holds exactly 4096 cached tokens and some exactly 2048. `page_ids`: each row lists 32 different pages in ascending order, all below the number of pages that hold the sequence's cached tokens, and always the last of those pages. `expert_ids`: each row names 8 different experts; over all rows no expert is named by more than 24 rows, a bound that some block reaches.
All inputs are finite; a program needn't handle non-finite values.
Results may differ from a plain program's by a relative error of at most 0.025.
Values may be sent and summed in bfloat16 or wider, within the bound.
No kernel may reach another device: no remote copies, remote signals or barrier semaphores. Data moves between devices by JAX's collectives and lax.ppermute only.
A program may use at most 128 MiB of HBM per device.

v0:
```python
import math
import jax
import jax.numpy as jnp
from jax import lax
from jax.sharding import PartitionSpec as P

D = 4096
EXPERTS = 64
NEG_FILL = -1e30
NORM_EPS = 1e-06


def copy_for_each(shard, axis):
    copies = jnp.broadcast_to(shard, (lax.axis_size(axis), *shard.shape))
    return lax.all_to_all(copies, axis, split_axis=0, concat_axis=0, tiled=True)


def in_order(pieces, dim):
    lengths = list(pieces.shape[1:])
    lengths[dim] *= pieces.shape[0]
    return jnp.moveaxis(pieces, 0, dim).reshape(lengths)


def gathered_copies(shard, axis, dim):
    pieces = copy_for_each(shard, axis)
    return in_order(pieces, dim)


def from_partner(shard, axis, distance):
    return lax.ppermute(shard, axis, [(i, i ^ 1 << distance) for i in range(lax.axis_size(axis))])


def taken_together(shard, axis):
    return copy_for_each(shard, axis).astype(jnp.float32).sum(axis=0)


def of_everyone(shard, axis):
    return copy_for_each(shard, axis).sum(axis=0)


def merge_pair(first, second):
    first_max, first_sum, first_acc = first
    second_max, second_sum, second_acc = second
    joined = jnp.maximum(first_max, second_max)
    first_factor = jnp.exp(first_max - joined)
    second_factor = jnp.exp(second_max - joined)
    return (
        joined,
        first_sum * first_factor + second_sum * second_factor,
        first_acc * first_factor[..., None] + second_acc * second_factor[..., None],
    )


def head_slice(partial_value, begin_at, span_size):
    return tuple(
        (lax.dynamic_slice_in_dim(member, begin_at, span_size, 1) for member in partial_value)
    )


def on_device(
    queries,
    newest_key_value,
    page_cache,
    lengths,
    page_ids,
    out_weight,
    residual,
    norm_gain,
    expert_ids,
    route_weight,
    gate_up_weight,
    down_weight,
):
    seq_count = queries.shape[0]
    head_dim = newest_key_value.shape[2] // 2
    kv_heads = newest_key_value.shape[1]
    sect_size = lax.axis_size("sect")
    head_size = lax.axis_size("head")
    batch_size = lax.axis_size("batch")
    group_size = sect_size * head_size // kv_heads
    position = lax.axis_index("sect") * head_size + lax.axis_index("head")
    kv_index = position // group_size
    quarter = position % group_size
    local_pages = page_cache.shape[1]
    page_len = page_cache.shape[2]
    scaling = 1.0 / math.sqrt(head_dim)
    all_heads = lax.all_gather(queries, "head", axis=1, tiled=True)
    kv_local = kv_index % (kv_heads // sect_size)
    group_query = lax.dynamic_slice_in_dim(all_heads, kv_local * head_dim, head_dim, 2)
    heads_dev = all_heads.shape[1] // group_size
    block_cols = heads_dev * head_dim
    chosen = lax.dynamic_index_in_dim(page_ids, kv_index, 1, keepdims=False)
    leading_page = quarter * local_pages
    page_number = jnp.broadcast_to(
        leading_page + jnp.arange(local_pages, dtype=jnp.int32), (seq_count, local_pages)
    )
    page_used = jnp.any(chosen[:, :, None] == page_number[:, None, :], axis=1)
    token_place = (
        page_number[:, :, None] * page_len + jnp.arange(page_len, dtype=jnp.int32)[None, None, :]
    )
    key_count = page_cache.shape[1] * page_len
    usable_pages = (page_used[:, :, None] & (token_place < lengths[:, None, None])).reshape(
        seq_count, key_count
    )
    gathered_keys = page_cache[..., :head_dim].reshape(seq_count, key_count, head_dim)
    gathered_values = page_cache[..., head_dim:].reshape(seq_count, key_count, head_dim)
    scores = (
        jnp.einsum("shd,skd->shk", group_query, gathered_keys, preferred_element_type=jnp.float32)
        * scaling
    )
    scores = jnp.where(usable_pages[:, None, :], scores, NEG_FILL)
    newest_entry = lax.dynamic_index_in_dim(newest_key_value, kv_index, 1, keepdims=False)
    fresh_score = (
        jnp.einsum(
            "shd,sd->sh",
            group_query,
            newest_entry[:, :head_dim],
            preferred_element_type=jnp.float32,
        )
        * scaling
    )
    leading = quarter == 0
    fresh_score = jnp.where(leading, fresh_score, NEG_FILL)
    running_max = jnp.maximum(jnp.max(scores, axis=2), fresh_score)
    weights = jnp.where(usable_pages[:, None, :], jnp.exp(scores - running_max[..., None]), 0.0)
    fresh_weight = jnp.where(leading, jnp.exp(fresh_score - running_max), 0.0)
    running_sum = jnp.sum(weights, axis=2) + fresh_weight
    weighted = jnp.einsum(
        "shk,skd->shd",
        weights.astype(jnp.bfloat16),
        gathered_values,
        preferred_element_type=jnp.float32,
    )
    weighted = weighted + fresh_weight.astype(jnp.bfloat16).astype(jnp.float32)[
        ..., None
    ] * newest_entry[:, None, head_dim:].astype(jnp.float32)
    partial_value = (running_max, running_sum, weighted)
    bit_count = group_size.bit_length() - 1
    for bit_index in reversed(range(bit_count)):
        half_heads = partial_value[0].shape[1] // 2
        keep_half = quarter >> bit_index & 1
        kept = head_slice(partial_value, keep_half * half_heads, half_heads)
        sent = head_slice(partial_value, (1 - keep_half) * half_heads, half_heads)
        partner = from_partner(sent, "head", bit_index)
        partial_value = merge_pair(kept, partner)
    attention = (
        (partial_value[2] / partial_value[1][..., None])
        .reshape(seq_count, block_cols)
        .astype(jnp.bfloat16)
    )
    head_terms = jnp.dot(
        lax.all_gather(attention, "batch", axis=0, tiled=True),
        out_weight,
        preferred_element_type=jnp.float32,
    )
    projected = lax.psum(head_terms, ("sect", "head"))
    hidden_state = residual.astype(jnp.float32) + projected
    squares = lax.psum(jnp.sum(hidden_state * hidden_state, axis=1), "batch")
    inverse = lax.rsqrt(squares / D + NORM_EPS)
    normed = (hidden_state * inverse[:, None] * norm_gain[None, :]).astype(jnp.bfloat16)
    token_count, top_count = expert_ids.shape
    capacity = 2 * token_count * top_count // EXPERTS
    pair_local = gate_up_weight.shape[0]
    flat_ids = expert_ids.reshape(-1)
    one_hot = (flat_ids[:, None] == jnp.arange(EXPERTS, dtype=jnp.int32)[None, :]).astype(jnp.int32)
    earlier = jnp.cumsum(one_hot, axis=0) - one_hot
    rank_in = jnp.sum(earlier * one_hot, axis=1)
    sub_half = lax.axis_index("head") // (head_size // 2)
    pair_first = lax.axis_index("sect") * (batch_size * pair_local)
    local_pair = flat_ids // 2 - pair_first
    in_sect = (local_pair >= 0) & (local_pair < batch_size * pair_local)
    full_slot = (
        (local_pair // pair_local * 2 + flat_ids % 2) * pair_local + local_pair % pair_local
    ) * capacity + rank_in
    full_slot = jnp.where(in_sect, full_slot, -1)
    slot_dev = pair_local * capacity
    slot_total = batch_size * 2 * slot_dev
    send_count = batch_size * slot_dev
    matches = (
        full_slot.reshape(token_count, top_count)[None, :, :]
        == jnp.arange(slot_total, dtype=jnp.int32)[:, None, None]
    )
    selector_full = (
        jnp.any(matches, axis=2).astype(jnp.bfloat16).reshape(batch_size, 2, slot_dev, token_count)
    )
    selector = lax.dynamic_index_in_dim(selector_full, sub_half, 1, keepdims=False).reshape(
        send_count, token_count
    )
    coefficient = route_weight / jnp.sum(route_weight, axis=1, keepdims=True)
    combine_full = jnp.sum(jnp.where(matches, coefficient[None, :, :], 0.0), axis=2).T
    cols_dev = normed.shape[1]
    outgoing = jnp.dot(selector, normed, preferred_element_type=jnp.float32).astype(jnp.bfloat16)
    outgoing = outgoing.reshape(batch_size, pair_local, capacity, cols_dev)
    arrived = lax.all_to_all(outgoing, "batch", split_axis=0, concat_axis=3, tiled=True)[0]
    mixture = jnp.einsum(
        "ecd,edgf->ecgf", arrived, gate_up_weight, preferred_element_type=jnp.float32
    )
    activated = (jax.nn.silu(mixture[:, :, 0]) * mixture[:, :, 1]).astype(jnp.bfloat16)
    expert_part = jnp.einsum(
        "ecf,efd->ecd", activated, down_weight, preferred_element_type=jnp.float32
    )
    leaving = expert_part.reshape(1, slot_dev, batch_size, cols_dev)
    came_back = (
        lax.all_to_all(
            leaving.astype(jnp.bfloat16), "batch", split_axis=2, concat_axis=0, tiled=True
        )
        .astype(leaving.dtype)
        .reshape(send_count, cols_dev)
    )
    weights_used = lax.dynamic_index_in_dim(
        combine_full.reshape(token_count, batch_size, 2, slot_dev), sub_half, 2, keepdims=False
    )
    weights_used = weights_used.reshape(token_count, send_count)
    combined = jnp.dot(weights_used, came_back, preferred_element_type=jnp.float32)
    expert_mix = lax.psum(combined, ("sect", "head"))
    return (hidden_state + expert_mix).astype(jnp.bfloat16)


def solution(mesh):
    placed = (
        P("batch", "head", "sect"),
        P("batch", None, None),
        P("batch", ("sect", "head"), None, None),
        P("batch"),
        P("batch", None, None),
        P(("sect", "head"), "batch"),
        P(None, "batch"),
        P("batch"),
        P(),
        P(),
        P(("sect", "batch"), None, None, "head"),
        P(("sect", "batch"), "head", None),
    )
    return jax.shard_map(
        on_device, mesh=mesh, in_specs=placed, out_specs=P(None, "batch"), check_vma=False
    )
```

profile of v0, /device:TPU:32, one launch (start us, length us, event | category | flops | bytes accessed | tf_op | source)
XLA Modules:
  0.0 342.4 jit_solution(5951458100370429770)
XLA Ops:
  6.5 0.7 copy.66
  7.3 34.3 %all_gather.6 = bf16[6,16,256]{2,0,1:T(8,128)(2,1)S(1)} all-gather(bf16[6,2,256]{2,0,1:T(8,128)(2,1)S(1)} %copy.66), channel_id=1, replica_groups=mesh['sect'=2,'batch'=16,'head'=8] {'head'}, dimensions={1}, use_global_device_ids=true | all-gather | bytes 55296 | tf_op jit(solution)/shard_map/all_gather | solution.py:87
  41.6 0.7 constant_dynamic-slice_fusion.14
  42.3 0.2 compare_reduce_fusion
  42.5 0.1 and.72
  42.6 0.1 and.73
  42.9 3.2 fusion.49
  46.2 0.1 fusion.29
  46.4 1.3 fusion.50
  47.8 1.2 fusion.8
  49.1 2.0 collective-permute-start.4
  51.1 1.4 convolution_add_fusion
  52.5 0.1 collective-permute-start.1
  52.7 0.1 copy.69
  52.7 0.1 eq.65
  53.0 1.8 reduce-window.6
  54.8 0.3 slice_reduce_fusion
  55.1 0.1 fusion.13
  55.4 0.8 fusion.2
  56.2 0.2 copy.78
  56.6 3.2 collective-permute-start.2
  59.9 0.3 collective-permute-start.5
  60.3 3.3 collective-permute-start.3
  63.6 1.4 collective-permute-done.5
  65.0 0.5 collective-permute-done.3
  65.7 18.2 %all-gather = bf16[16,6,512]{2,1,0:T(8,128)(2,1)S(1)} all-gather(bf16[1,6,512]{2,1,0:T(8,128)(2,1)S(1)} %reshape.182), channel_id=1, replica_groups=mesh['sect'=2,'batch'=16,'head'=8] {'batch'}, dimensions={0}, use_global_device_ids=true | all-gather | bytes 104448 | tf_op jit(solution)/shard_map/all_gather | solution.py:152
  83.9 0.8 fusion.51
  84.8 94.1 %all-reduce.3.cloned.1.call-done = f32[96,256]{1,0:T(8,128)} async-done(((f32[96,256]{1,0:T(8,128)}), f32[96,256]{1,0:T(8,128)}) %all-reduce.3.cloned.1.call-update) | async-done | bytes 98320 | tf_op jit(solution)/shard_map/psum | solution.py:156
  178.9 1.0 multiply_reduce_fusion
  180.0 21.5 %psum.22 = f32[96]{0:T(128)S(1)} all-reduce(f32[96]{0:T(128)S(1)} %multiply_reduce_fusion), channel_id=1, replica_groups=mesh['sect'=2,'batch'=16,'head'=8] {'batch'}, use_global_device_ids=true, to_apply=%region_11.12 | all-reduce | flops 96 | bytes 768 | tf_op jit(solution)/shard_map/psum | solution.py:158
  201.4 1.8 convolution_convert_fusion.1
  203.3 9.6 %all-to-all-start = ((bf16[16,1,24,256]{3,2,1,0:T(8,128)(2,1)}), bf16[16,1,24,256]{3,2,1,0:T(8,128)(2,1)}, u32[]{:S(2)}, u32[]{:S(2)}) async-start(bf16[16,1,24,256]{3,2,1,0:T(8,128)(2,1)} %bitcast.13), calls=%async_computation | async-start | bytes 393216 | tf_op jit(solution)/shard_map/all_to_all | solution.py:194
  212.9 3.4 %copy.86 = bf16[4096,384]{1,0:T(8,128)(2,1)S(1)} copy(bf16[4096,384]{0,1:T(8,128)(2,1)} %bitcast.92) | data formatting | bytes 6291456 | tf_op jit(solution)/shard_map/ecf,efd->ecd/dot_general | solution.py:199
  216.3 0.6 reduce_sum.50
  216.9 4.6 %all-to-all-done = bf16[16,1,24,256]{3,2,1,0:T(8,128)(2,1)} async-done(((bf16[16,1,24,256]{3,2,1,0:T(8,128)(2,1)}), bf16[16,1,24,256]{3,2,1,0:T(8,128)(2,1)}, u32[]{:S(2)}, u32[]{:S(2)}) %all-to-all-start) | async-done | bytes 196640 | tf_op jit(solution)/shard_map/all_to_all | solution.py:194
  221.5 1.6 copy.80
  223.1 1.7 reshape.187
  224.8 3.8 %fusion.5 = f32[1,24,2,384]{3,1,2,0:T(8,128)S(1)} fusion(bf16[24,4096,1]{1,0,2:T(8,128)(2,1)} %reshape.187, bf16[4096,2,384]{2,1,0:T(2,128)(2,1)} %bitcast.102), kind=kOutput, calls=%fused_computation.10 | convolution fusion | flops 150994944 | bytes 6561792 | tf_op jit(solution)/shard_map/ecd,edgf->ecgf/dot_general | solution.py:195
  228.7 1.9 fusion.4
  230.6 4.8 %all-to-all-start.1 = ((bf16[1,24,16,256]{3,1,0,2:T(8,128)(2,1)}), bf16[1,24,16,256]{3,1,0,2:T(8,128)(2,1)S(1)}, u32[]{:S(2)}, u32[]{:S(2)}) async-start(bf16[1,24,16,256]{3,1,0,2:T(8,128)(2,1)} %fusion.4), calls=%async_computation.1 | async-start | bytes 393216 | tf_op jit(solution)/shard_map/all_to_all | solution.py:204
  235.4 0.7 broadcast_divide_fusion
  236.1 0.1 copy.76
  236.2 1.6 select_reduce_fusion
  237.8 0.2 copy.77
  238.0 5.8 %all-to-all-done.1 = bf16[1,24,16,256]{3,1,0,2:T(8,128)(2,1)S(1)} async-done(((bf16[1,24,16,256]{3,1,0,2:T(8,128)(2,1)}), bf16[1,24,16,256]{3,1,0,2:T(8,128)(2,1)S(1)}, u32[]{:S(2)}, u32[]{:S(2)}) %all-to-all-start.1) | async-done | bytes 196640 | tf_op jit(solution)/shard_map/all_to_all | solution.py:204
  243.8 0.8 fusion.52
  244.7 89.4 %all-reduce.5.cloned.1.call-done = f32[96,256]{1,0:T(8,128)} async-done(((f32[96,256]{1,0:T(8,128)}), f32[96,256]{1,0:T(8,128)}) %all-reduce.5.cloned.1.call-update) | async-done | bytes 98320 | tf_op jit(solution)/shard_map/psum | solution.py:215
  334.0 1.5 add_convert_fusion
  (58 shorter events, 1.4 us)
Async XLA Ops:
  6.5 77.4 %copy-start = (bf16[512,256]{1,0:T(8,128)(2,1)S(1)}, bf16[512,256]{1,0:T(8,128)(2,1)}, u32[]{:S(2)}) copy-start(bf16[512,256]{1,0:T(8,128)(2,1)} %param.17) | copy-start | bytes 786436
  6.5 172.4 %all-reduce.3.cloned.1.call-start = ((), (), s32[]{:S(2)}) async-start(), calls=%async_computation.2 | async-start | bytes 196608 | tf_op jit(solution)/shard_map/psum | solution.py:156
  42.9 3.2 copy-start.6
  42.9 3.4 %copy-start.8 = (s32[6]{0:T(128)S(1)}, s32[6]{0:T(128)}, u32[]{:S(2)}) copy-start(s32[6]{0:T(128)} %param.15) | copy-start | bytes 76
  46.2 6.5 %copy-start.5 = (s32[96,8]{0,1:T(8,128)S(1)}, s32[96,8]{0,1:T(8,128)}, u32[]{:S(2)}) copy-start(s32[96,8]{0,1:T(8,128)} %param.20) | copy-start | bytes 9220
  47.7 8.7 %collective-permute-start = (f32[6,8]{1,0:T(8,128)S(1)}, f32[6,8]{1,0:T(8,128)S(1)}, u32[]{:S(2)}, u32[]{:S(2)}) collective-permute-start(f32[6,8]{1,0:T(8,128)S(1)} %constant_dynamic-slice_fusion.10), channel_id=1, source_target_pairs={{0,2},{1,3},{2,0},{3,1},{4,6},{5,7},{6,4},{7,5},{8,10},{9,11},{10,... | collective-permute-start | bytes 584 | tf_op jit(solution)/shard_map/ppermute | solution.py:30
  49.1 7.3 %collective-permute-start.4 = (f32[6,8]{1,0:T(8,128)S(1)}, f32[6,8]{1,0:T(8,128)S(1)}, u32[]{:S(2)}, u32[]{:S(2)}) collective-permute-start(f32[6,8]{1,0:T(8,128)S(1)} %constant_dynamic-slice_fusion.4), channel_id=1, source_target_pairs={{0,2},{1,3},{2,0},{3,1},{4,6},{5,7},{6,4},{7,5},{8,10},{9,11},{10,... | collective-permute-start | bytes 584 | tf_op jit(solution)/shard_map/ppermute | solution.py:30
  51.1 127.8 %copy-start.2 = (bf16[96,256]{1,0:T(8,128)(2,1)S(1)}, bf16[96,256]{1,0:T(8,128)(2,1)}, u32[]{:S(2)}) copy-start(bf16[96,256]{1,0:T(8,128)(2,1)} %param.18) | copy-start | bytes 147460
  51.1 150.3 %copy-start.7 = (f32[256]{0:T(256)S(1)}, f32[256]{0:T(256)}, u32[]{:S(2)}) copy-start(f32[256]{0:T(256)} %param.19) | copy-start | bytes 3076
  52.5 7.7 %collective-permute-start.1 = (f32[6,8,128]{2,1,0:T(8,128)S(1)}, f32[6,8,128]{2,1,0:T(8,128)S(1)}, u32[]{:S(2)}, u32[]{:S(2)}) collective-permute-start(f32[6,8,128]{2,1,0:T(8,128)S(1)} %constant_dynamic-slice_fusion.9), channel_id=1, source_target_pairs={{0,2},{1,3},{2,0},{3,1},{4,6},{5,7},{6,4},{7,5},{8,10},{9,11},{10,... | collective-permute-start | bytes 73736 | tf_op jit(solution)/shard_map/ppermute | solution.py:30
  55.4 157.5 %copy-start.3 = (s32[96,8]{1,0:T(8,128)}, s32[96,8]{1,0:T(8,128)S(1)}, u32[]{:S(2)}) copy-start(s32[96,8]{1,0:T(8,128)S(1)} %fusion.22) | copy-start | bytes 9220
  56.6 7.0 %collective-permute-start.2 = (f32[6,4]{1,0:T(8,128)S(1)}, f32[6,4]{1,0:T(8,128)S(1)}, u32[]{:S(2)}, u32[]{:S(2)}) collective-permute-start(f32[6,4]{1,0:T(8,128)S(1)} %constant_dynamic-slice_fusion.7), channel_id=1, source_target_pairs={{0,1},{1,0},{2,3},{3,2},{4,5},{5,4},{6,7},{7,6},{8,9},{9,8},{10,11... | collective-permute-start | bytes 296 | tf_op jit(solution)/shard_map/ppermute | solution.py:30
  59.9 5.1 %collective-permute-start.5 = (f32[6,4]{1,0:T(8,128)S(1)}, f32[6,4]{1,0:T(8,128)S(1)}, u32[]{:S(2)}, u32[]{:S(2)}) collective-permute-start(f32[6,4]{1,0:T(8,128)S(1)} %constant_dynamic-slice_fusion.2), channel_id=1, source_target_pairs={{0,1},{1,0},{2,3},{3,2},{4,5},{5,4},{6,7},{7,6},{8,9},{9,8},{10,11... | collective-permute-start | bytes 296 | tf_op jit(solution)/shard_map/ppermute | solution.py:30
  60.3 5.3 %collective-permute-start.3 = (f32[6,4,128]{2,1,0:T(4,128)S(1)}, f32[6,4,128]{2,1,0:T(4,128)S(1)}, u32[]{:S(2)}, u32[]{:S(2)}) collective-permute-start(f32[6,4,128]{2,1,0:T(4,128)S(1)} %constant_dynamic-slice_fusion.6), channel_id=1, source_target_pairs={{0,1},{1,0},{2,3},{3,2},{4,5},{5,4},{6,7},{7,6},{8,9},{9,8},{10,11... | collective-permute-start | bytes 36872 | tf_op jit(solution)/shard_map/ppermute | solution.py:30
  203.3 18.2 %all-to-all-start = ((bf16[16,1,24,256]{3,2,1,0:T(8,128)(2,1)}), bf16[16,1,24,256]{3,2,1,0:T(8,128)(2,1)}, u32[]{:S(2)}, u32[]{:S(2)}) async-start(bf16[16,1,24,256]{3,2,1,0:T(8,128)(2,1)} %bitcast.13), calls=%async_computation | async-start | bytes 393216 | tf_op jit(solution)/shard_map/all_to_all | solution.py:194
  212.9 3.4 %copy-start.4 = (f32[96,8]{0,1:T(8,128)S(1)}, f32[96,8]{0,1:T(8,128)}, u32[]{:S(2)}) copy-start(f32[96,8]{0,1:T(8,128)} %param.21) | copy-start | bytes 9220
  228.7 105.4 %copy-start.1 = (f32[96,256]{1,0:T(8,128)S(1)}, f32[96,256]{1,0:T(8,128)}, u32[]{:S(2)}) copy-start(f32[96,256]{1,0:T(8,128)} %all-reduce.3.cloned.1.call-done) | copy-start | bytes 294916
  230.6 13.3 %all-to-all-start.1 = ((bf16[1,24,16,256]{3,1,0,2:T(8,128)(2,1)}), bf16[1,24,16,256]{3,1,0,2:T(8,128)(2,1)S(1)}, u32[]{:S(2)}, u32[]{:S(2)}) async-start(bf16[1,24,16,256]{3,1,0,2:T(8,128)(2,1)} %fusion.4), calls=%async_computation.1 | async-start | bytes 393216 | tf_op jit(solution)/shard_map/all_to_all | solution.py:204
  235.3 98.7 %all-reduce.5.cloned.1.call-start = ((), (), s32[]{:S(2)}) async-start(), calls=%async_computation.3 | async-start | bytes 196608 | tf_op jit(solution)/shard_map/psum | solution.py:215
Sparse Core Ops, SparseCore 0:
  84.9 94.0 all-reduce.2
  244.8 89.1 all-reduce.4
where the time goes:
time: 343 us; the launch traced here: 342 us
  waiting for transfers between devices  196 us (57%)
  blocking collectives  73.9 us (22%)
  starting transfers between devices  23.4 us (7%)
  between operations  13.7 us (4%)
  local copies, waits for them, and re-layouts  13.3 us (4%)
  matrix products  12 us (3%)
  other arithmetic  10.2 us (3%)
    psum x1, waiting for transfers between devices, on_device(): projected = lax.psum(head_terms, ('sect', 'head'))  94.1 us
    psum x1, waiting for transfers between devices, on_device(): expert_mix = lax.psum(combined, ('sect', 'head'))  89.4 us
    all_gather x1, blocking collectives, on_device(): all_heads = lax.all_gather(queries, 'head', axis=1, tiled=True)  34.3 us
    psum x1, blocking collectives, on_device(): squares = lax.psum(jnp.sum(hidden_state * hidden_state, axis=1), 'batch')  21.5 us
    all_gather x1, blocking collectives, on_device(): lax.all_gather(attention, 'batch', axis=0, tiled=True)  18.2 us
    all_to_all x1, starting transfers between devices, on_device(): lax.all_to_all(outgoing, 'batch', split_axis=0, concat_axis=3, tiled=True)  9.58 us
    ppermute x6, starting transfers between devices, from_partner(): lax.ppermute(shard, axis, [(i, i ^ 1 << distance) for i in range(lax.axis...  9.03 us
  transfers between devices with their start and end apart: 10, of which 6 were waited for; matrix products, arithmetic and copies ran while one was open for 4% of the time, Pallas kernels for 0%

commit v1 on v0

--- a/solution.py
+++ b/solution.py
@@ -8,6 +8,18 @@
 EXPERTS = 64
 NEG_FILL = -1e30
 NORM_EPS = 1e-06
+
+
+def update_hubs_all(x0, net_axis):
+    return jnp.concatenate(
+        lax.all_to_all(
+            jnp.stack(lax.axis_size(net_axis) * [x0]),
+            axis_name=net_axis,
+            split_axis=0,
+            concat_axis=0,
+        ),
+        axis=1,
+    )
 
 
 def copy_for_each(shard, axis):
@@ -84,7 +96,7 @@
     local_pages = page_cache.shape[1]
     page_len = page_cache.shape[2]
     scaling = 1.0 / math.sqrt(head_dim)
-    all_heads = lax.all_gather(queries, "head", axis=1, tiled=True)
+    all_heads = update_hubs_all(queries, "head")
     kv_local = kv_index % (kv_heads // sect_size)
     group_query = lax.dynamic_slice_in_dim(all_heads, kv_local * head_dim, head_dim, 2)
     heads_dev = all_heads.shape[1] // group_size

time: 343 us -> 326 us (0.950)
  blocking collectives: 73.9 us -> 39.7 us
  starting transfers between devices: 23.4 us -> 32.1 us
  other arithmetic: 10.2 us -> 15.4 us
  local copies, waits for them, and re-layouts: 13.3 us -> 18 us
    all_gather x1 -> x0, blocking collectives: 34.3 us -> none  [on_device(): all_heads = lax.all_gather(queries, 'head', axis=1, tiled=True)]
    all_to_all x0 -> x1, starting transfers between devices: none -> 6.93 us  [update_hubs_all(): lax.all_to_all(jnp.stack(lax.axis_size(net_axis) * [x0]), axis_name=net_a...]
  transfers between devices with their start and end apart: 10 -> 11, of which waited for: 6 -> 7; matrix products, arithmetic and copies ran while one was open for 4% -> 8% of each run, Pallas kernels for 0% -> 0%
where the time goes in v1:
time: 326 us; the launch traced here: 325 us
  waiting for transfers between devices  195 us (60%)
  blocking collectives  39.7 us (12%)
  starting transfers between devices  32.1 us (10%)
  local copies, waits for them, and re-layouts  18 us (6%)
  other arithmetic  15.4 us (5%)
  between operations  13.7 us (4%)
  matrix products  11.1 us (3%)
    psum x1, waiting for transfers between devices, on_device(): projected = lax.psum(head_terms, ('sect', 'head'))  92.6 us
    psum x1, waiting for transfers between devices, on_device(): expert_mix = lax.psum(combined, ('sect', 'head'))  89.4 us
    psum x1, blocking collectives, on_device(): squares = lax.psum(jnp.sum(hidden_state * hidden_state, axis=1), 'batch')  21.5 us
    all_gather x1, blocking collectives, on_device(): lax.all_gather(attention, 'batch', axis=0, tiled=True)  18.2 us
    ppermute x6, starting transfers between devices, from_partner(): lax.ppermute(shard, axis, [(i, i ^ 1 << distance) for i in range(lax.axis...  10.7 us
    all_to_all x1, starting transfers between devices, on_device(): lax.all_to_all(outgoing, 'batch', split_axis=0, concat_axis=3, tiled=True)  9.58 us
    all_to_all x1, starting transfers between devices, update_hubs_all(): lax.all_to_all(jnp.stack(lax.axis_size(net_axis) * [x0]), axis_name=net_a...  6.93 us
  transfers between devices with their start and end apart: 11, of which 7 were waited for; matrix products, arithmetic and copies ran while one was open for 8% of the time, Pallas kernels for 0%

profile of v1, /device:TPU:32, one launch (start us, length us, event | category | flops | bytes accessed | tf_op | source)
XLA Modules:
  0.0 324.9 jit_solution(17558469268169185940)
XLA Ops:
  6.5 1.4 stack.2
  7.9 6.9 %all-to-all-start = ((bf16[8,6,2,256]{3,2,1,0:T(2,128)(2,1)}), bf16[8,6,2,256]{3,2,1,0:T(2,128)(2,1)S(1)}, u32[]{:S(2)}, u32[]{:S(2)}) async-start(bf16[8,6,2,256]{3,2,1,0:T(2,128)(2,1)} %stack.2), calls=%async_computation | async-start | bytes 98304 | tf_op jit(solution)/shard_map/all_to_all | solution.py:15
  14.9 0.8 copy.66
  15.9 0.7 constant_dynamic-slice_fusion.12
  16.6 0.6 slice_convert_fusion
  17.2 0.7 constant_dynamic-slice_fusion.13
  18.5 3.2 fusion.51
  21.7 0.7 fusion.16
  22.4 4.4 %reduce-window.6 = s32[64,6,128]{2,0,1:T(8,128)} reduce-window(s32[64,6,128]{2,0,1:T(8,128)} %fusion.16, s32[]{:T(128)} %constant.119.clone.1), window={size=1x1x128 pad=0_0x0_0x127_0}, to_apply=%region_4.5 | reduce-window | flops 6242304 | bytes 393220 | tf_op jit(solution)/shard_map/reduce-window
  26.8 1.2 slice_reduce_fusion
  28.0 1.1 fusion.13
  29.1 0.7 reduce_sum.49
  29.8 0.9 fusion.22
  30.8 0.5 copy-done.3
  31.3 0.8 fusion.2
  32.1 0.8 copy.75
  33.1 0.6 fusion.52
  33.8 2.0 collective-permute-start
  35.8 0.9 fusion.8
  36.9 1.1 convolution_add_fusion
  38.1 2.0 collective-permute-start.1
  40.1 0.4 collective-permute-done.4
  40.6 3.0 collective-permute-start.2
  43.7 0.6 collective-permute-start.5
  44.3 3.1 collective-permute-start.3
  47.4 1.4 collective-permute-done.5
  48.9 0.8 collective-permute-done.3
  49.7 18.2 %all-gather = bf16[16,6,512]{2,1,0:T(8,128)(2,1)S(1)} all-gather(bf16[1,6,512]{2,1,0:T(8,128)(2,1)S(1)} %reshape.192), channel_id=1, replica_groups=mesh['sect'=2,'batch'=16,'head'=8] {'batch'}, dimensions={0}, use_global_device_ids=true | all-gather | bytes 104448 | tf_op jit(solution)/shard_map/all_gather | solution.py:164
  68.0 0.8 fusion.53
  68.9 92.6 %all-reduce.3.cloned.1.call-done = f32[96,256]{1,0:T(8,128)} async-done(((f32[96,256]{1,0:T(8,128)}), f32[96,256]{1,0:T(8,128)}) %all-reduce.3.cloned.1.call-update) | async-done | bytes 98320 | tf_op jit(solution)/shard_map/psum | solution.py:168
  161.5 1.0 multiply_reduce_fusion
  162.5 21.5 %psum.22 = f32[96]{0:T(128)S(1)} all-reduce(f32[96]{0:T(128)S(1)} %multiply_reduce_fusion), channel_id=1, replica_groups=mesh['sect'=2,'batch'=16,'head'=8] {'batch'}, use_global_device_ids=true, to_apply=%region_11.12 | all-reduce | flops 96 | bytes 768 | tf_op jit(solution)/shard_map/psum | solution.py:170
  184.0 1.8 convolution_convert_fusion.1
  185.8 9.6 %all-to-all-start.1 = ((bf16[16,1,24,256]{3,2,1,0:T(8,128)(2,1)}), bf16[16,1,24,256]{3,2,1,0:T(8,128)(2,1)}, u32[]{:S(2)}, u32[]{:S(2)}) async-start(bf16[16,1,24,256]{3,2,1,0:T(8,128)(2,1)} %bitcast.14), calls=%async_computation.1 | async-start | bytes 393216 | tf_op jit(solution)/shard_map/all_to_all | solution.py:206
  195.4 3.4 %copy.83 = bf16[4096,384]{1,0:T(8,128)(2,1)S(1)} copy(bf16[4096,384]{0,1:T(8,128)(2,1)} %bitcast.93) | data formatting | bytes 6291456 | tf_op jit(solution)/shard_map/ecf,efd->ecd/dot_general | solution.py:211
  198.8 0.6 reduce_sum.50
  199.4 4.6 %all-to-all-done.1 = bf16[16,1,24,256]{3,2,1,0:T(8,128)(2,1)} async-done(((bf16[16,1,24,256]{3,2,1,0:T(8,128)(2,1)}), bf16[16,1,24,256]{3,2,1,0:T(8,128)(2,1)}, u32[]{:S(2)}, u32[]{:S(2)}) %all-to-all-start.1) | async-done | bytes 196640 | tf_op jit(solution)/shard_map/all_to_all | solution.py:206
  204.0 1.6 copy.77
  205.7 1.7 reshape.197
  207.4 3.8 %fusion.5 = f32[1,24,2,384]{3,1,2,0:T(8,128)S(1)} fusion(bf16[24,4096,1]{1,0,2:T(8,128)(2,1)} %reshape.197, bf16[4096,2,384]{2,1,0:T(2,128)(2,1)} %bitcast.104), kind=kOutput, calls=%fused_computation.10 | convolution fusion | flops 150994944 | bytes 6561792 | tf_op jit(solution)/shard_map/ecd,edgf->ecgf/dot_general | solution.py:207
  211.2 1.9 fusion.4
  213.1 4.8 %all-to-all-start.2 = ((bf16[1,24,16,256]{3,1,0,2:T(8,128)(2,1)}), bf16[1,24,16,256]{3,1,0,2:T(8,128)(2,1)S(1)}, u32[]{:S(2)}, u32[]{:S(2)}) async-start(bf16[1,24,16,256]{3,1,0,2:T(8,128)(2,1)} %fusion.4), calls=%async_computation.2 | async-start | bytes 393216 | tf_op jit(solution)/shard_map/all_to_all | solution.py:216
  217.9 0.7 broadcast_divide_fusion
  218.7 1.6 select_reduce_fusion
  220.5 5.8 %all-to-all-done.2 = bf16[1,24,16,256]{3,1,0,2:T(8,128)(2,1)S(1)} async-done(((bf16[1,24,16,256]{3,1,0,2:T(8,128)(2,1)}), bf16[1,24,16,256]{3,1,0,2:T(8,128)(2,1)S(1)}, u32[]{:S(2)}, u32[]{:S(2)}) %all-to-all-start.2) | async-done | bytes 196640 | tf_op jit(solution)/shard_map/all_to_all | solution.py:216
  226.3 0.8 fusion.54
  227.2 89.4 %all-reduce.5.cloned.1.call-done = f32[96,256]{1,0:T(8,128)} async-done(((f32[96,256]{1,0:T(8,128)}), f32[96,256]{1,0:T(8,128)}) %all-reduce.5.cloned.1.call-update) | async-done | bytes 98320 | tf_op jit(solution)/shard_map/psum | solution.py:227
  316.6 1.5 add_convert_fusion
  (60 shorter events, 2.3 us)
Async XLA Ops:
  6.5 61.4 %copy-start = (bf16[512,256]{1,0:T(8,128)(2,1)S(1)}, bf16[512,256]{1,0:T(8,128)(2,1)}, u32[]{:S(2)}) copy-start(bf16[512,256]{1,0:T(8,128)(2,1)} %param.17) | copy-start | bytes 786436
  7.9 25.0 %all-to-all-start = ((bf16[8,6,2,256]{3,2,1,0:T(2,128)(2,1)}), bf16[8,6,2,256]{3,2,1,0:T(2,128)(2,1)S(1)}, u32[]{:S(2)}, u32[]{:S(2)}) async-start(bf16[8,6,2,256]{3,2,1,0:T(2,128)(2,1)} %stack.2), calls=%async_computation | async-start | bytes 98304 | tf_op jit(solution)/shard_map/all_to_all | solution.py:15
  14.8 146.6 %all-reduce.3.cloned.1.call-start = ((), (), s32[]{:S(2)}) async-start(), calls=%async_computation.3 | async-start | bytes 196608 | tf_op jit(solution)/shard_map/psum | solution.py:168
  18.5 12.1 %copy-start.8 = (s32[6]{0:T(128)S(1)}, s32[6]{0:T(128)}, u32[]{:S(2)}) copy-start(s32[6]{0:T(128)} %param.15) | copy-start | bytes 76
  30.7 0.6 copy-start.3
  31.3 1.8 copy-start.5
  33.7 35.1 %copy-start.4 = (pred[768,96]{1,0:T(8,128)(4,1)S(1)}, pred[768,96]{1,0:T(8,128)(4,1)}, u32[]{:S(2)}) copy-start(pred[768,96]{1,0:T(8,128)(4,1)} %copy.75) | copy-start | bytes 221188
  33.7 127.7 %copy-start.2 = (bf16[96,256]{1,0:T(8,128)(2,1)S(1)}, bf16[96,256]{1,0:T(8,128)(2,1)}, u32[]{:S(2)}) copy-start(bf16[96,256]{1,0:T(8,128)(2,1)} %param.18) | copy-start | bytes 147460
  33.7 150.2 %copy-start.7 = (f32[256]{0:T(256)S(1)}, f32[256]{0:T(256)}, u32[]{:S(2)}) copy-start(f32[256]{0:T(256)} %param.19) | copy-start | bytes 3076
  33.8 6.2 %collective-permute-start = (f32[6,8]{1,0:T(8,128)S(1)}, f32[6,8]{1,0:T(8,128)S(1)}, u32[]{:S(2)}, u32[]{:S(2)}) collective-permute-start(f32[6,8]{1,0:T(8,128)S(1)} %constant_dynamic-slice_fusion.10), channel_id=1, source_target_pairs={{0,2},{1,3},{2,0},{3,1},{4,6},{5,7},{6,4},{7,5},{8,10},{9,11},{10,... | collective-permute-start | bytes 584 | tf_op jit(solution)/shard_map/ppermute | solution.py:42
  36.8 3.6 %collective-permute-start.4 = (f32[6,8]{1,0:T(8,128)S(1)}, f32[6,8]{1,0:T(8,128)S(1)}, u32[]{:S(2)}, u32[]{:S(2)}) collective-permute-start(f32[6,8]{1,0:T(8,128)S(1)} %constant_dynamic-slice_fusion.4), channel_id=1, source_target_pairs={{0,2},{1,3},{2,0},{3,1},{4,6},{5,7},{6,4},{7,5},{8,10},{9,11},{10,... | collective-permute-start | bytes 584 | tf_op jit(solution)/shard_map/ppermute | solution.py:42
  38.1 6.2 %collective-permute-start.1 = (f32[6,8,128]{2,1,0:T(8,128)S(1)}, f32[6,8,128]{2,1,0:T(8,128)S(1)}, u32[]{:S(2)}, u32[]{:S(2)}) collective-permute-start(f32[6,8,128]{2,1,0:T(8,128)S(1)} %constant_dynamic-slice_fusion.9), channel_id=1, source_target_pairs={{0,2},{1,3},{2,0},{3,1},{4,6},{5,7},{6,4},{7,5},{8,10},{9,11},{10,... | collective-permute-start | bytes 73736 | tf_op jit(solution)/shard_map/ppermute | solution.py:42
  40.6 6.8 %collective-permute-start.2 = (f32[6,4]{1,0:T(8,128)S(1)}, f32[6,4]{1,0:T(8,128)S(1)}, u32[]{:S(2)}, u32[]{:S(2)}) collective-permute-start(f32[6,4]{1,0:T(8,128)S(1)} %constant_dynamic-slice_fusion.7), channel_id=1, source_target_pairs={{0,1},{1,0},{2,3},{3,2},{4,5},{5,4},{6,7},{7,6},{8,9},{9,8},{10,11... | collective-permute-start | bytes 296 | tf_op jit(solution)/shard_map/ppermute | solution.py:42
  43.7 5.1 %collective-permute-start.5 = (f32[6,4]{1,0:T(8,128)S(1)}, f32[6,4]{1,0:T(8,128)S(1)}, u32[]{:S(2)}, u32[]{:S(2)}) collective-permute-start(f32[6,4]{1,0:T(8,128)S(1)} %constant_dynamic-slice_fusion.2), channel_id=1, source_target_pairs={{0,1},{1,0},{2,3},{3,2},{4,5},{5,4},{6,7},{7,6},{8,9},{9,8},{10,11... | collective-permute-start | bytes 296 | tf_op jit(solution)/shard_map/ppermute | solution.py:42
  44.3 5.3 %collective-permute-start.3 = (f32[6,4,128]{2,1,0:T(4,128)S(1)}, f32[6,4,128]{2,1,0:T(4,128)S(1)}, u32[]{:S(2)}, u32[]{:S(2)}) collective-permute-start(f32[6,4,128]{2,1,0:T(4,128)S(1)} %constant_dynamic-slice_fusion.6), channel_id=1, source_target_pairs={{0,1},{1,0},{2,3},{3,2},{4,5},{5,4},{6,7},{7,6},{8,9},{9,8},{10,11... | collective-permute-start | bytes 36872 | tf_op jit(solution)/shard_map/ppermute | solution.py:42
  185.8 18.2 %all-to-all-start.1 = ((bf16[16,1,24,256]{3,2,1,0:T(8,128)(2,1)}), bf16[16,1,24,256]{3,2,1,0:T(8,128)(2,1)}, u32[]{:S(2)}, u32[]{:S(2)}) async-start(bf16[16,1,24,256]{3,2,1,0:T(8,128)(2,1)} %bitcast.14), calls=%async_computation.1 | async-start | bytes 393216 | tf_op jit(solution)/shard_map/all_to_all | solution.py:206
  195.4 3.4 %copy-start.6 = (f32[96,8]{0,1:T(8,128)S(1)}, f32[96,8]{0,1:T(8,128)}, u32[]{:S(2)}) copy-start(f32[96,8]{0,1:T(8,128)} %param.21) | copy-start | bytes 9220
  211.2 105.4 %copy-start.1 = (f32[96,256]{1,0:T(8,128)S(1)}, f32[96,256]{1,0:T(8,128)}, u32[]{:S(2)}) copy-start(f32[96,256]{1,0:T(8,128)} %all-reduce.3.cloned.1.call-done) | copy-start | bytes 294916
  213.1 13.3 %all-to-all-start.2 = ((bf16[1,24,16,256]{3,1,0,2:T(8,128)(2,1)}), bf16[1,24,16,256]{3,1,0,2:T(8,128)(2,1)S(1)}, u32[]{:S(2)}, u32[]{:S(2)}) async-start(bf16[1,24,16,256]{3,1,0,2:T(8,128)(2,1)} %fusion.4), calls=%async_computation.2 | async-start | bytes 393216 | tf_op jit(solution)/shard_map/all_to_all | solution.py:216
  217.8 98.7 %all-reduce.5.cloned.1.call-start = ((), (), s32[]{:S(2)}) async-start(), calls=%async_computation.4 | async-start | bytes 196608 | tf_op jit(solution)/shard_map/psum | solution.py:227
Sparse Core Ops, SparseCore 0:
  69.0 92.4 all-reduce.2
  227.3 89.1 all-reduce.4
